TPU v7x, 512 devices: a whole 4x8x8 slice. The times are simulated.
512 devices in a mesh: req: 64 (over y, x, core), tp: 8 (over z).
Axes of the slice: x: 4, y: 8, z: 8, core: 2. Of those that a mesh axis runs over, the one named last changes fastest.
Arguments:
- hidden: bfloat16 [2048, 5, 2560], P('req', None, 'tp'), may hold values from -6 to 6
- norm_gain: bfloat16 [2560], replicated, may hold values from 0.099609375 to 1.8984375
- query_weight: bfloat16 [2560, 2560], P(None, 'tp'), may hold values from -0.125 to 0.125
- key_value_matrix: bfloat16 [2560, 8, 160], P(None, 'tp'), may hold values from -0.125 to 0.125
- output_weight: bfloat16 [2560, 2560], P('tp'), may hold values from -0.5 to 0.5
- key_value_cache: bfloat16 [2048, 64, 8, 160], P('req', None, 'tp'), as said below
- deal_order: int32 [2048], P('req'), may hold values from 0 to 2047, as said below
- cache_length: int32 [2048], P('req'), may hold values from 1 to 64, as said below
- accepted: int32 [2048], P('req'), may hold values from 1 to 5
Outputs:
- block_output: bfloat16 [2048, 5, 2560], P('req', None, 'tp')
- new_entries: bfloat16 [2048, 5, 8, 160], P('req', None, 'tp')
Inputs may be any that keep to these rules, and one draw needn't show every extreme that they name: deal_order is a permutation of the 2048 requests; slot i lies on index i // 32 of req, and request r arrives on index r // 32. Every index deals at most 1 of its requests to any one index, and exactly 1 to each of 32 indices. Cache entries of slot i at positions from cache_length[i] on are unused. `key_value_cache`: at positions below cache_length[i] the first 80 entries of each head are the keys, already rotated for their positions, and the last 80 the values.
All inputs are finite; a program needn't handle non-finite values.
Results may differ from a plain program's by a relative error of at most 0.0091.
Values may be sent and summed in bfloat16 or wider, within the bound.
No kernel may reach another device: no remote copies, remote signals or barrier semaphores. Data moves between devices by JAX's collectives and lax.ppermute only.
A program may use at most 128 MiB of HBM per device.

v0:
```python
import math
import jax
import jax.numpy as jnp
from jax import lax
from jax.sharding import PartitionSpec as P

HEAD_SIZE = 80
masked_score = -1e30


def rotate(values, positions):
    half_dim = HEAD_SIZE // 2
    frequency = 10000.0 ** (-2.0 * jnp.arange(half_dim, dtype=jnp.float32) / HEAD_SIZE)
    angles = positions.astype(jnp.float32)[..., None] * frequency
    cosine_part = jnp.cos(angles)
    sine_part = jnp.sin(angles)
    first_half = values[..., :half_dim]
    second_half = values[..., half_dim:]
    return jnp.concatenate(
        [
            first_half * cosine_part - second_half * sine_part,
            second_half * cosine_part + first_half * sine_part,
        ],
        axis=-1,
    )


def attend(query_rows, key_value_cache, fresh, cache_length):
    scale = 1.0 / math.sqrt(HEAD_SIZE)
    slot_count = query_rows.shape[0]
    verified = query_rows.shape[1]
    cache_keys = key_value_cache[..., :HEAD_SIZE]
    cache_values = key_value_cache[..., HEAD_SIZE:]
    fresh_keys = fresh[..., :HEAD_SIZE]
    fresh_values = fresh[..., HEAD_SIZE:]
    cache_scores = (
        jnp.einsum("rtghd,rcgd->rghtc", query_rows, cache_keys, preferred_element_type=jnp.float32)
        * scale
    )
    visible = jnp.arange(key_value_cache.shape[1], dtype=jnp.int32)[None, :] < cache_length[:, None]
    cache_scores = jnp.where(visible[:, None, None, None, :], cache_scores, masked_score)
    fresh_scores = (
        jnp.einsum("rtghd,rugd->rghtu", query_rows, fresh_keys, preferred_element_type=jnp.float32)
        * scale
    )
    causal = (
        jnp.arange(verified, dtype=jnp.int32)[:, None]
        >= jnp.arange(verified, dtype=jnp.int32)[None, :]
    )
    fresh_scores = jnp.where(causal[None, None, None, :, :], fresh_scores, masked_score)
    largest = jnp.maximum(jnp.max(cache_scores, axis=-1), jnp.max(fresh_scores, axis=-1))[..., None]
    cache_expos = jnp.exp(cache_scores - largest)
    fresh_expos = jnp.exp(fresh_scores - largest)
    totals = jnp.sum(cache_expos, axis=-1, keepdims=True) + jnp.sum(
        fresh_expos, axis=-1, keepdims=True
    )
    cache_weights = (cache_expos / totals).astype(jnp.bfloat16)
    fresh_weights = (fresh_expos / totals).astype(jnp.bfloat16)
    mixed = jnp.einsum(
        "rghtc,rcgd->rtghd", cache_weights, cache_values, preferred_element_type=jnp.float32
    )
    mixed = mixed + jnp.einsum(
        "rghtu,rugd->rtghd", fresh_weights, fresh_values, preferred_element_type=jnp.float32
    )
    return mixed.astype(jnp.bfloat16).reshape(slot_count, verified, -1)


def body(
    hidden,
    norm_gain,
    query_weight,
    key_value_matrix,
    output_weight,
    key_value_cache,
    deal_order,
    cache_length,
    accepted,
):
    slot_count = deal_order.shape[0]
    verified = hidden.shape[1]
    device_index = lax.axis_index("req")
    my_requests = device_index * slot_count + jnp.arange(slot_count, dtype=jnp.int32)
    piece = lax.all_gather(hidden, "req", axis=0, tiled=True)
    picker = (deal_order[:, None] == jnp.arange(piece.shape[0], dtype=jnp.int32)[None, :]).astype(
        jnp.bfloat16
    )
    dealt_rows = jnp.einsum(
        "in,ntf->itf", picker, piece, preferred_element_type=jnp.float32
    ).astype(jnp.bfloat16)
    features = lax.all_gather(dealt_rows, "tp", axis=2, tiled=True)
    widened = features.astype(jnp.float32)
    variance = jnp.mean(widened * widened, axis=-1, keepdims=True)
    normed = (widened * lax.rsqrt(variance + 1e-05) * norm_gain.astype(jnp.float32)).astype(
        jnp.bfloat16
    )
    heads_here = query_weight.shape[1] // HEAD_SIZE
    groups_here = key_value_matrix.shape[1]
    positions = cache_length[:, None] + jnp.arange(verified, dtype=jnp.int32)[None, :]
    query_rows = jnp.einsum("rtd,de->rte", normed, query_weight, preferred_element_type=jnp.float32)
    query_rows = query_rows.reshape(
        slot_count, verified, groups_here, heads_here // groups_here, HEAD_SIZE
    )
    query_rows = rotate(query_rows, positions[:, :, None, None]).astype(jnp.bfloat16)
    projected = jnp.einsum(
        "rtd,dge->rtge", normed, key_value_matrix, preferred_element_type=jnp.float32
    )
    fresh = jnp.concatenate(
        [rotate(projected[..., :HEAD_SIZE], positions[:, :, None]), projected[..., HEAD_SIZE:]],
        axis=-1,
    ).astype(jnp.bfloat16)
    keep = (jnp.arange(verified, dtype=jnp.int32)[None, :] < accepted[:, None])[:, :, None, None]
    new_entries = jnp.where(keep, fresh, jnp.zeros_like(fresh))
    mixed = attend(query_rows, key_value_cache, fresh, cache_length)
    partial_sum = jnp.einsum(
        "rte,ed->rtd", mixed, output_weight, preferred_element_type=jnp.float32
    )
    out_dealt = lax.psum_scatter(partial_sum, "tp", scatter_dimension=2, tiled=True).astype(
        jnp.bfloat16
    )
    piece_rows = lax.all_gather(out_dealt, "req", axis=0, tiled=True)
    piece_owners = lax.all_gather(deal_order, "req", axis=0, tiled=True)
    picker = (my_requests[:, None] == piece_owners[None, :]).astype(jnp.bfloat16)
    block_output = jnp.einsum(
        "jn,ntf->jtf", picker, piece_rows, preferred_element_type=jnp.float32
    ).astype(jnp.bfloat16)
    return (block_output, new_entries)


def solution(mesh):
    placed = (
        P("req", None, "tp"),
        P(),
        P(None, "tp"),
        P(None, "tp", None),
        P("tp", None),
        P("req", None, "tp", None),
        P("req"),
        P("req"),
        P("req"),
    )
    return jax.shard_map(
        body,
        mesh=mesh,
        in_specs=placed,
        out_specs=(P("req", None, "tp"), P("req", None, "tp", None)),
        check_vma=False,
    )
```

profile of v0, /device:TPU:1, one launch (start us, length us, event | category | flops | bytes accessed | tf_op | source)
XLA Modules:
  0.0 338.5 jit_solution(15841835390689357700)
XLA Ops:
  7.2 0.7 all-gather.3.cloned.1.call-update
  8.0 0.7 convert_element_type.71
  8.7 0.7 add_convert_fusion
  9.4 0.7 iota_compare_fusion.1
  10.7 93.9 %all-gather.3.cloned.1.call-done = bf16[2048,5,320]{2,0,1:T(8,128)(2,1)} async-done(((bf16[32,5,320]{2,0,1:T(8,128)(2,1)}), bf16[2048,5,320]{2,0,1:T(8,128)(2,1)}) %all-gather.3.cloned.1.call-update) | async-done | bytes 6553616 | tf_op jit(solution)/shard_map/all_gather | solution.py:83
  104.6 4.7 %convolution_convert_fusion.1 = bf16[32,5,320]{2,0,1:T(8,128)(2,1)S(1)} fusion(bf16[2048,5,320]{2,0,1:T(8,128)(2,1)} %all-gather.3.cloned.1.call-done, s32[32]{0:T(128)} %param.15), kind=kOutput, calls=%fused_computation.21 | convolution fusion | flops 209831936 | bytes 6656128 | tf_op jit(solution)/shard_map/in,ntf->itf/dot_general | solution.py:87
  109.7 55.1 %all_gather.14 = bf16[32,5,2560]{0,1,2:T(8,128)(2,1)} all-gather(bf16[32,5,320]{0,1,2:T(8,128)(2,1)S(1)} %copy.43), channel_id=1, replica_groups=mesh['req'=64,'tp'=8] {'tp'}, dimensions={2}, use_global_device_ids=true | all-gather | bytes 921600 | tf_op jit(solution)/shard_map/all_gather | solution.py:90
  164.9 4.4 %copy.44 = bf16[32,5,2560]{2,0,1:T(8,128)(2,1)S(1)} copy(bf16[32,5,2560]{0,1,2:T(8,128)(2,1)} %all_gather.14) | data formatting | bytes 1638400 | tf_op jit(solution)/shard_map/all_gather | solution.py:90
  169.5 1.7 convolution_bitcast_fusion.1
  172.3 0.8 fusion.5
  174.1 1.4 fusion.51
  176.8 0.8 convolution_bitcast_fusion
  178.2 0.6 fusion.3
  178.8 5.5 %copy.64 = f32[32,5,2560]{0,1,2:T(8,128)} copy(f32[32,5,2560]{2,0,1:T(8,128)S(1)} %fusion.3) | data formatting | bytes 3276800
  184.3 8.0 %reshape.347 = f32[2560,160]{1,0:T(8,128)} reshape(f32[2560,5,32]{2,1,0:T(8,128)} %bitcast.87) | data formatting | bytes 3276800
  192.4 39.6 %reduce-scatter.4.cloned.1.call-done = f32[320,160]{1,0:T(8,128)} async-done(((f32[2560,160]{1,0:T(8,128)}), f32[320,160]{1,0:T(8,128)}) %reduce-scatter.4.cloned.1.call-update) | async-done | bytes 204816
  232.1 1.2 reshape.348
  233.3 1.0 copy.65
  234.3 1.3 dynamic-slice
  236.5 21.3 %all-reduce = s32[2048]{0:T(1024)S(1)} all-reduce(s32[2048]{0:T(1024)S(1)} %dynamic-update-slice), channel_id=1, replica_groups=mesh['req'=64,'tp'=8] {'req'}, use_global_device_ids=true, to_apply=%add | all-reduce | flops 2048 | bytes 16384
  257.9 1.0 slice.51
  258.9 0.8 fusion.44
  259.7 67.0 %all-gather.5.cloned.1.call-done = bf16[2048,5,320]{2,0,1:T(8,128)(2,1)} async-done(((bf16[32,5,320]{2,0,1:T(8,128)(2,1)}), bf16[2048,5,320]{2,0,1:T(8,128)(2,1)}) %all-gather.5.cloned.1.call-update) | async-done | bytes 6553616 | tf_op jit(solution)/shard_map/all_gather | solution.py:120
  326.7 5.3 %convolution_convert_fusion = bf16[32,5,320]{2,0,1:T(8,128)(2,1)} fusion(bf16[2048,5,320]{2,0,1:T(8,128)(2,1)} %all-gather.5.cloned.1.call-done, s32[2048]{0:T(1024)S(1)} %all-reduce, s32[32]{0:T(128)S(1)} %iota_add_fusion), kind=kOutput, calls=%fused_computation.20 | convolution fusion | flops 209831936 | bytes 6664320 | tf_op jit(solution)/shard_map/jn,ntf->jtf/dot_general | solution.py:123
  (42 shorter events, 5.7 us)
Async XLA Ops:
  7.2 171.1 %copy-start = (bf16[320,2560]{1,0:T(8,128)(2,1)S(1)}, bf16[320,2560]{1,0:T(8,128)(2,1)}, u32[]{:S(2)}) copy-start(bf16[320,2560]{1,0:T(8,128)(2,1)} %param.13) | copy-start | bytes 4915204
  7.2 97.5 %all-gather.3.cloned.1.call-start = ((), (), s32[]{:S(2)}) async-start(), calls=%async_computation.1 | async-start | bytes 7987200 | tf_op jit(solution)/shard_map/all_gather | solution.py:83
  7.9 224.2 %reduce-scatter.4.cloned.1.call-start = ((), (), s32[]{:S(2)}) async-start(), calls=%async_computation.3 | async-start | bytes 2949120
  169.2 3.0 copy-start.4
  171.2 0.7 copy-start.1
  173.5 1.9 copy-start.2
  192.4 43.9 %copy-start.3 = (s32[32]{0:T(128)S(1)}, s32[32]{0:T(128)}, u32[]{:S(2)}) copy-start(s32[32]{0:T(128)} %param.15) | copy-start | bytes 388
  192.4 65.5 %copy-start.5 = (s32[32]{0:T(128)S(1)}, s32[32]{0:T(128)}, u32[]{:S(2)}) copy-start(s32[32]{0:T(128)} %param.17) | copy-start | bytes 388
  192.4 134.3 %all-gather.5.cloned.1.call-start = ((), (), s32[]{:S(2)}) async-start(), calls=%async_computation.2 | async-start | bytes 7987200 | tf_op jit(solution)/shard_map/all_gather | solution.py:120
Sparse Core Ops, SparseCore 0:
  11.3 93.2 all-gather.2
  192.5 39.5 reduce-scatter.3
  235.9 90.6 all-gather.4
where the time goes:
time: 339 us; the launch traced here: 338 us
  waiting for transfers between devices  201 us (59%)
  blocking collectives  76.4 us (23%)
  local copies, waits for them, and re-layouts  24.5 us (7%)
  matrix products  16.2 us (5%)
  between operations  14.6 us (4%)
  other arithmetic  5.35 us (2%)
    all_gather x1, waiting for transfers between devices, body(): piece = lax.all_gather(hidden, 'req', axis=0, tiled=True)  93.9 us
    all_gather x1, waiting for transfers between devices, body(): piece_rows = lax.all_gather(out_dealt, 'req', axis=0, tiled=True)  67 us
    all_gather x1, blocking collectives, body(): features = lax.all_gather(dealt_rows, 'tp', axis=2, tiled=True)  55.1 us
    unnamed x4, waiting for transfers between devices  40.3 us
    unnamed x1, blocking collectives  21.3 us
    unnamed x19, local copies, waits for them, and re-layouts  17.9 us
  transfers between devices with their start and end apart: 3, of which 3 were waited for; matrix products, arithmetic and copies ran while one was open for 2% of the time, Pallas kernels for 0%

commit v1 on v0

--- a/solution.py
+++ b/solution.py
@@ -80,7 +80,9 @@
     verified = hidden.shape[1]
     device_index = lax.axis_index("req")
     my_requests = device_index * slot_count + jnp.arange(slot_count, dtype=jnp.int32)
-    piece = lax.all_gather(hidden, "req", axis=0, tiled=True)
+    piece = jnp.concatenate(
+        lax.all_to_all(jnp.stack([hidden] * lax.axis_size("req")), "req", 0, 0), axis=0
+    )
     picker = (deal_order[:, None] == jnp.arange(piece.shape[0], dtype=jnp.int32)[None, :]).astype(
         jnp.bfloat16
     )

time: 339 us -> 437 us (1.29)
  waiting for transfers between devices: 201 us -> 279 us
  starting transfers between devices: 0.12 us -> 12.2 us
  local copies, waits for them, and re-layouts: 24.5 us -> 32.9 us
    all_to_all x0 -> x1, waiting for transfers between devices: none -> 169 us  [body(): lax.all_to_all(jnp.stack([hidden] * lax.axis_size('req')), 'req', 0, 0)]
    all_gather x1 -> x0, waiting for transfers between devices: 93.9 us -> none  [body(): piece = lax.all_gather(hidden, 'req', axis=0, tiled=True)]
    all_to_all x0 -> x1, starting transfers between devices: none -> 12.1 us  [body(): lax.all_to_all(jnp.stack([hidden] * lax.axis_size('req')), 'req', 0, 0)]
    another operation x1 -> x2, local copies, waits for them, and re-layouts: 0.08 us -> 4.94 us  [the longest x1 4.86 us: body(): jnp.stack([hidden] * lax.axis_size('req'))]
    unnamed x4 -> x3, waiting for transfers between devices: 40.3 us -> 42.9 us
    unnamed x19 -> x27, local copies, waits for them, and re-layouts: 17.9 us -> 17.3 us
  transfers between devices with their start and end apart: 3 -> 3, of which waited for: 3 -> 3; matrix products, arithmetic and copies ran while one was open for 2% -> 1% of each run, Pallas kernels for 0% -> 0%
where the time goes in v1:
time: 437 us
  waiting for transfers between devices  279 us (64%)
  blocking collectives  78.8 us (18%)
  local copies, waits for them, and re-layouts  32.9 us (8%)
  between operations  15 us (3%)
  matrix products  13.6 us (3%)
  starting transfers between devices  12.2 us (3%)
  other arithmetic  4.53 us (1%)
    all_to_all x1, waiting for transfers between devices, body(): lax.all_to_all(jnp.stack([hidden] * lax.axis_size('req')), 'req', 0, 0)  169 us
    all_gather x1, waiting for transfers between devices, body(): piece_rows = lax.all_gather(out_dealt, 'req', axis=0, tiled=True)  67.2 us
    all_gather x1, blocking collectives, body(): features = lax.all_gather(dealt_rows, 'tp', axis=2, tiled=True)  57.8 us
    unnamed x3, waiting for transfers between devices  42.9 us
    unnamed x1, blocking collectives  21 us
    unnamed x27, local copies, waits for them, and re-layouts  17.3 us
    all_to_all x1, starting transfers between devices, body(): lax.all_to_all(jnp.stack([hidden] * lax.axis_size('req')), 'req', 0, 0)  12.1 us
  transfers between devices with their start and end apart: 3, of which 3 were waited for; matrix products, arithmetic and copies ran while one was open for 1% of the time, Pallas kernels for 0%

profile of v1, /device:TPU:1, one launch (start us, length us, event | category | flops | bytes accessed | tf_op | source)
XLA Modules:
  0.0 436.5 jit_solution(15037796194475624628)
XLA Ops:
  7.2 4.9 %stack.2 = bf16[64,32,5,320]{3,1,2,0:T(8,128)(2,1)} broadcast(bf16[32,5,320]{2,0,1:T(8,128)(2,1)} %param.9), dimensions={1,2,3} | broadcast | bytes 6656000 | tf_op jit(solution)/shard_map/stack | solution.py:84
  12.0 12.1 %all-to-all-start = ((bf16[64,32,5,320]{3,1,2,0:T(8,128)(2,1)}), bf16[64,32,5,320]{3,1,2,0:T(8,128)(2,1)}, u32[]{:S(2)}, u32[]{:S(2)}) async-start(bf16[64,32,5,320]{3,1,2,0:T(8,128)(2,1)} %stack.2), calls=%async_computation | async-start | bytes 15728640 | tf_op jit(solution)/shard_map/all_to_all | solution.py:84
  24.2 0.6 convert_element_type.71
  26.1 169.3 %all-to-all-done = bf16[64,32,5,320]{3,1,2,0:T(8,128)(2,1)} async-done(((bf16[64,32,5,320]{3,1,2,0:T(8,128)(2,1)}), bf16[64,32,5,320]{3,1,2,0:T(8,128)(2,1)}, u32[]{:S(2)}, u32[]{:S(2)}) %all-to-all-start) | async-done | bytes 6553632 | tf_op jit(solution)/shard_map/all_to_all | solution.py:84
  195.4 4.2 copy.47
  199.6 2.1 convolution_convert_fusion.1
  202.1 57.8 %all_gather.10 = bf16[32,5,2560]{0,1,2:T(8,128)(2,1)} all-gather(bf16[32,5,320]{0,1,2:T(8,128)(2,1)S(1)} %copy.49), channel_id=1, replica_groups=mesh['req'=64,'tp'=8] {'tp'}, dimensions={2}, use_global_device_ids=true | all-gather | bytes 921600 | tf_op jit(solution)/shard_map/all_gather | solution.py:92
  259.9 4.4 %copy.50 = bf16[32,5,2560]{2,0,1:T(8,128)(2,1)S(1)} copy(bf16[32,5,2560]{0,1,2:T(8,128)(2,1)} %all_gather.10) | data formatting | bytes 1638400 | tf_op jit(solution)/shard_map/all_gather | solution.py:92
  264.6 1.7 convolution_bitcast_fusion.1
  266.8 0.8 fusion.5
  268.7 1.4 fusion.51
  271.4 0.8 convolution_bitcast_fusion
  272.8 0.6 fusion.3
  273.4 5.5 %copy.71 = f32[32,5,2560]{0,1,2:T(8,128)} copy(f32[32,5,2560]{2,0,1:T(8,128)S(1)} %fusion.3) | data formatting | bytes 3276800
  278.9 8.0 %reshape.353 = f32[2560,160]{1,0:T(8,128)} reshape(f32[2560,5,32]{2,1,0:T(8,128)} %bitcast.88) | data formatting | bytes 3276800
  287.0 42.9 %reduce-scatter.4.cloned.1.call-done = f32[320,160]{1,0:T(8,128)} async-done(((f32[2560,160]{1,0:T(8,128)}), f32[320,160]{1,0:T(8,128)}) %reduce-scatter.4.cloned.1.call-update) | async-done | bytes 204816
  329.8 1.2 reshape.354
  331.1 1.0 copy.72
  332.1 1.3 dynamic-slice
  334.3 21.0 %all-reduce = s32[2048]{0:T(1024)S(1)} all-reduce(s32[2048]{0:T(1024)S(1)} %dynamic-update-slice), channel_id=1, replica_groups=mesh['req'=64,'tp'=8] {'req'}, use_global_device_ids=true, to_apply=%add | all-reduce | flops 2048 | bytes 16384
  355.3 1.0 slice.51
  356.3 0.8 fusion.44
  357.1 67.2 %all-gather.2.cloned.1.call-done = bf16[2048,5,320]{2,0,1:T(8,128)(2,1)} async-done(((bf16[32,5,320]{2,0,1:T(8,128)(2,1)}), bf16[2048,5,320]{2,0,1:T(8,128)(2,1)}) %all-gather.2.cloned.1.call-update) | async-done | bytes 6553616 | tf_op jit(solution)/shard_map/all_gather | solution.py:122
  424.4 5.3 %convolution_convert_fusion = bf16[32,5,320]{2,0,1:T(8,128)(2,1)} fusion(bf16[2048,5,320]{2,0,1:T(8,128)(2,1)} %all-gather.2.cloned.1.call-done, s32[2048]{0:T(1024)S(1)} %all-reduce, s32[32]{0:T(128)S(1)} %iota_add_fusion), kind=kOutput, calls=%fused_computation.20 | convolution fusion | flops 209831936 | bytes 6664320 | tf_op jit(solution)/shard_map/jn,ntf->jtf/dot_general | solution.py:125
  (51 shorter events, 5.8 us)
Async XLA Ops:
  7.2 265.6 %copy-start = (bf16[320,2560]{1,0:T(8,128)(2,1)S(1)}, bf16[320,2560]{1,0:T(8,128)(2,1)}, u32[]{:S(2)}) copy-start(bf16[320,2560]{1,0:T(8,128)(2,1)} %param.13) | copy-start | bytes 4915204
  12.0 12.2 %copy-start.4 = (bf16[2560]{0:T(1024)(128)(2,1)S(1)}, bf16[2560]{0:T(1024)(128)(2,1)}, u32[]{:S(2)}) copy-start(bf16[2560]{0:T(1024)(128)(2,1)} %param.10) | copy-start | bytes 15364
  12.0 12.8 %copy-start.5 = (s32[32]{0:T(128)S(1)}, s32[32]{0:T(128)}, u32[]{:S(2)}) copy-start(s32[32]{0:T(128)} %param.16) | copy-start | bytes 388
  12.0 183.4 %all-to-all-start = ((bf16[64,32,5,320]{3,1,2,0:T(8,128)(2,1)}), bf16[64,32,5,320]{3,1,2,0:T(8,128)(2,1)}, u32[]{:S(2)}, u32[]{:S(2)}) async-start(bf16[64,32,5,320]{3,1,2,0:T(8,128)(2,1)} %stack.2), calls=%async_computation | async-start | bytes 15728640 | tf_op jit(solution)/shard_map/all_to_all | solution.py:84
  24.1 305.7 %reduce-scatter.4.cloned.1.call-start = ((), (), s32[]{:S(2)}) async-start(), calls=%async_computation.3 | async-start | bytes 2949120
  259.9 4.6 %copy-start.3 = (f32[2560]{0:T(1024)S(1)}, f32[2560]{0:T(1024)}, u32[]{:S(2)}) copy-start(f32[2560]{0:T(1024)} %convert_element_type.71) | copy-start | bytes 30724
  264.3 2.5 copy-start.8
  266.3 1.3 copy-start.1
  267.6 1.1 copy-start.6
  268.1 2.0 copy-start.2
  286.9 47.1 %copy-start.7 = (s32[32]{0:T(128)S(1)}, s32[32]{0:T(128)}, u32[]{:S(2)}) copy-start(s32[32]{0:T(128)} %param.15) | copy-start | bytes 388
  286.9 68.4 %copy-start.9 = (s32[32]{0:T(128)S(1)}, s32[32]{0:T(128)}, u32[]{:S(2)}) copy-start(s32[32]{0:T(128)} %param.17) | copy-start | bytes 388
  286.9 137.4 %all-gather.2.cloned.1.call-start = ((), (), s32[]{:S(2)}) async-start(), calls=%async_computation.2 | async-start | bytes 7987200 | tf_op jit(solution)/shard_map/all_gather | solution.py:122
Sparse Core Ops, SparseCore 0:
  287.0 42.7 reduce-scatter.3
  333.7 90.6 all-gather.1
